TPU v7x, 128 devices: a whole 4x4x4 slice. The times are simulated.
128 devices in a mesh: req: 16 (over z, y), tensor: 8 (over x, core).
Axes of the slice: x: 4, y: 4, z: 4, core: 2. Of those that a mesh axis runs over, the one named last changes fastest.
Arguments:
- residual_input: bfloat16 [8192, 7168], P('req', 'tensor'), may hold values from -6 to 6
- input_norm_gain: float32 [7168], replicated, may hold values from 0.25 to 1.75
- query_weight: bfloat16 [7168, 4096], P(None, 'tensor'), may hold values from -0.09375 to 0.09375
- key_value_weight: bfloat16 [7168, 2048], P(None, 'tensor'), may hold values from -0.09375 to 0.09375
- output_weight: bfloat16 [4096, 7168], P('tensor'), may hold values from -0.375 to 0.375
- adapter_down_maps: bfloat16 [64, 48, 7168], P('req', None, 'tensor'), may hold values from -0.0625 to 0.0625
- adapter_query_up: bfloat16 [64, 16, 4096], P('req', None, 'tensor'), may hold values from -0.375 to 0.375
- adapter_key_value_up: bfloat16 [64, 2, 16, 1024], P('req', None, None, 'tensor'), may hold values from -0.375 to 0.375
- adapter_output_down: bfloat16 [64, 16, 4096], P('req', None, 'tensor'), may hold values from -0.375 to 0.375
- adapter_output_up: bfloat16 [64, 16, 7168], P('req', None, 'tensor'), may hold values from -0.375 to 0.375
- request_adapter: int32 [64], P('req'), may hold values from 0 to 63
- prompt_length: int32 [64], P('req'), may hold values from 32 to 128, as said below
- cache_length: int32 [32], replicated, may hold values from 16 to 2048, as said below
- first_page_device: int32 [32], replicated, may hold values from 0 to 15
- page_slot_table: int32 [16, 32], P('req'), may hold values from 0 to 31, as said below
- cache_page_pool: bfloat16 [512, 128, 2048], P('req', None, 'tensor'), may hold values from -200 to 200
Outputs:
- block_out: bfloat16 [8192, 7168], P('req', 'tensor')
Inputs may be any that keep to these rules, and one draw needn't show every extreme that they name: `prompt_length`: some request in every draw fills all 128 rows of its block. `cache_length`: some cache in every draw has 2048 positions. `page_slot_table`: each row is a permutation of the cached requests over the pool slots of one device.
All inputs are finite; a program needn't handle non-finite values.
Results may differ from a plain program's by a relative error of at most 0.035.
Values may be sent and summed in bfloat16 or wider, within the bound.
No kernel may reach another device: no remote copies, remote signals or barrier semaphores. Data moves between devices by JAX's collectives and lax.ppermute only.
A program may use at most 128 MiB of HBM per device.

v0:
```python
import jax
import jax.numpy as jnp
from jax import lax
from jax.sharding import PartitionSpec as P

HEAD_SIZE = 128
ROPE_BASE = 5000000.0
ADAPTER_SCALE = 2.0
EPSILON = 1e-05
NEG_FILL = -1e30


def rotate(vectors, positions):
    half_dim = vectors.shape[-1] // 2
    frequency = ROPE_BASE ** (-jnp.arange(half_dim, dtype=jnp.float32) / half_dim)
    angles = positions.astype(jnp.float32)[..., None] * frequency
    cosine = jnp.cos(angles)
    sine_part = jnp.sin(angles)
    front_half = vectors[..., :half_dim]
    back_half = vectors[..., half_dim:]
    return jnp.concatenate(
        [front_half * cosine - back_half * sine_part, back_half * cosine + front_half * sine_part],
        axis=-1,
    )


def partial_softmax(query_rows, key_rows, value_rows, allowed):
    score_scale = query_rows.shape[-1] ** (-0.5)
    scores = (
        jnp.einsum("bsvgd,bkvd->bvsgk", query_rows, key_rows, preferred_element_type=jnp.float32)
        * score_scale
    )
    spread_mask = allowed[:, None, :, None, :]
    scores = jnp.where(spread_mask, scores, NEG_FILL)
    peak_scores = jnp.max(scores, axis=-1)
    weights = jnp.where(spread_mask, jnp.exp(scores - peak_scores[..., None]), 0.0)
    totals = jnp.sum(weights, axis=-1)
    summed = jnp.einsum(
        "bvsgk,bkvd->bvsgd",
        weights.astype(jnp.bfloat16),
        value_rows,
        preferred_element_type=jnp.float32,
    )
    return (peak_scores, totals, summed)


def local(
    residual_input,
    input_norm_gain,
    query_weight,
    key_value_weight,
    output_weight,
    adapter_down_maps,
    adapter_query_up,
    adapter_key_value_up,
    adapter_output_down,
    adapter_output_up,
    request_adapter,
    prompt_length,
    cache_length,
    first_page_device,
    page_slot_table,
    cache_page_pool,
):
    holders = lax.axis_size("req")
    req_index = lax.axis_index("req")
    tensor_index = lax.axis_index("tensor")
    request_number = request_adapter.shape[0]
    cached_count = request_number // 2
    row_count = residual_input.shape[0]
    request_slot_rows = row_count // request_number
    piece_width = residual_input.shape[1]
    local_kv = key_value_weight.shape[1] // (2 * HEAD_SIZE)
    group_size = query_weight.shape[1] // (HEAD_SIZE * local_kv)
    page_rows = cache_page_pool.shape[1]
    gathered = lax.all_gather(residual_input, "tensor", axis=1, tiled=True)
    widened = gathered.astype(jnp.float32)
    inverse = lax.rsqrt(jnp.mean(widened * widened, axis=1, keepdims=True) + EPSILON)
    normed = (widened * inverse * input_norm_gain).astype(jnp.bfloat16)
    empty_sel = tuple(
        (
            jnp.zeros((request_number,) + adapter_lookup.shape[1:], jnp.bfloat16)
            for adapter_lookup in (
                adapter_down_maps,
                adapter_query_up,
                adapter_key_value_up,
                adapter_output_down,
                adapter_output_up,
            )
        )
    )
    pieces = (
        lax.all_gather(adapter_down_maps, "req", axis=0, tiled=True),
        lax.all_gather(adapter_query_up, "req", axis=0, tiled=True),
        lax.all_gather(adapter_key_value_up, "req", axis=0, tiled=True),
        lax.all_gather(adapter_output_down, "req", axis=0, tiled=True),
        lax.all_gather(adapter_output_up, "req", axis=0, tiled=True),
    )
    block_count = pieces[0].shape[0]
    adapter_ids = jnp.arange(block_count, dtype=jnp.int32)
    onehot = (request_adapter[:, None] == adapter_ids[None, :]).astype(jnp.bfloat16)
    down_picked, query_picked, key_value_picked, output_down_picked, oup_sel = tuple(
        (
            jnp.dot(onehot, segment.reshape(block_count, -1), preferred_element_type=jnp.float32)
            .reshape(held_sel.shape)
            .astype(jnp.bfloat16)
            for held_sel, segment in zip(empty_sel, pieces)
        )
    )
    adapter_rank_size = query_picked.shape[1]
    own_columns = lax.dynamic_slice_in_dim(
        normed, tensor_index * piece_width, piece_width, 1
    ).reshape(request_number, request_slot_rows, piece_width)
    partial_low = jnp.einsum(
        "rsd,rkd->rsk", own_columns, down_picked, preferred_element_type=jnp.float32
    )
    reduced_input = (
        lax.psum(partial_low.reshape(-1, 128).astype(jnp.bfloat16), "tensor")
        .astype(jnp.float32)
        .reshape(request_number, request_slot_rows, 3 * adapter_rank_size)
        .astype(jnp.bfloat16)
    )
    query_rows = jnp.dot(normed, query_weight, preferred_element_type=jnp.float32).reshape(
        request_number, request_slot_rows, -1
    )
    query_rows = query_rows + ADAPTER_SCALE * jnp.einsum(
        "ibm,imf->ibf",
        reduced_input[..., :adapter_rank_size],
        query_picked,
        preferred_element_type=jnp.float32,
    )
    keyval = jnp.dot(normed, key_value_weight, preferred_element_type=jnp.float32).reshape(
        request_number, request_slot_rows, local_kv, 2 * HEAD_SIZE
    )
    key_add = jnp.einsum(
        "ibm,imf->ibf",
        reduced_input[..., adapter_rank_size : 2 * adapter_rank_size],
        key_value_picked[:, 0],
        preferred_element_type=jnp.float32,
    ).reshape(request_number, request_slot_rows, local_kv, HEAD_SIZE)
    value_add = jnp.einsum(
        "ibm,imf->ibf",
        reduced_input[..., 2 * adapter_rank_size :],
        key_value_picked[:, 1],
        preferred_element_type=jnp.float32,
    ).reshape(request_number, request_slot_rows, local_kv, HEAD_SIZE)
    my_cache = lax.dynamic_slice_in_dim(cache_length, req_index * cached_count, cached_count, 0)
    offsets = jnp.stack([jnp.zeros_like(my_cache), my_cache], axis=1).reshape(request_number)
    slot_index = jnp.arange(request_slot_rows, dtype=jnp.int32)
    positions = offsets[:, None] + slot_index[None, :]
    query_rot = rotate(
        query_rows.reshape(request_number, request_slot_rows, local_kv, group_size, HEAD_SIZE),
        positions[:, :, None, None],
    ).astype(jnp.bfloat16)
    key_rot = rotate(keyval[..., :HEAD_SIZE] + key_add, positions[:, :, None]).astype(jnp.bfloat16)
    value_new = (keyval[..., HEAD_SIZE:] + value_add).astype(jnp.bfloat16)
    causal = slot_index[None, :, None] >= slot_index[None, None, :]
    own_mask = causal & (slot_index[None, None, :] < prompt_length[:, None, None])
    own_part = partial_softmax(query_rot, key_rot, value_new, own_mask)
    asked_queries = query_rot[1::2]
    slot_order = page_slot_table[0].reshape(holders, cached_count).T.reshape(-1)
    outgoing = cache_page_pool[slot_order].reshape(
        cached_count, holders, page_rows, cache_page_pool.shape[2]
    )
    arrived = lax.all_to_all(outgoing, "req", split_axis=1, concat_axis=1, tiled=True)
    my_base = lax.dynamic_slice_in_dim(first_page_device, req_index * cached_count, cached_count, 0)
    page_of = (jnp.arange(holders, dtype=jnp.int32)[None, :] - my_base[:, None]) % holders
    key_pos = (
        page_of[:, :, None] * page_rows + jnp.arange(page_rows, dtype=jnp.int32)[None, None, :]
    ).reshape(cached_count, holders * page_rows)
    entries = arrived.reshape(cached_count, holders * page_rows, local_kv, 2 * HEAD_SIZE)
    visible = jnp.broadcast_to(
        (key_pos < my_cache[:, None])[:, None, :],
        (cached_count, request_slot_rows, holders * page_rows),
    )
    cache_part = partial_softmax(
        asked_queries, entries[..., :HEAD_SIZE], entries[..., HEAD_SIZE:], visible
    )
    filler = jnp.full_like(cache_part[0], NEG_FILL)
    spread_peak = jnp.stack([filler, cache_part[0]], axis=1).reshape(own_part[0].shape)
    spread_total = jnp.stack([jnp.zeros_like(cache_part[1]), cache_part[1]], axis=1).reshape(
        own_part[1].shape
    )
    spread_sum = jnp.stack([jnp.zeros_like(cache_part[2]), cache_part[2]], axis=1).reshape(
        own_part[2].shape
    )
    highest_all = jnp.maximum(own_part[0], spread_peak)
    own_weight = jnp.exp(own_part[0] - highest_all)
    cache_weight = jnp.exp(spread_peak - highest_all)
    denominator = own_part[1] * own_weight + spread_total * cache_weight
    numerator = own_part[2] * own_weight[..., None] + spread_sum * cache_weight[..., None]
    live_rows = slot_index[None, :] < prompt_length[:, None]
    attended = jnp.where(
        live_rows[:, None, :, None, None], numerator / denominator[..., None], 0.0
    ).astype(jnp.bfloat16)
    attended = jnp.transpose(attended, (0, 2, 1, 3, 4)).reshape(row_count, -1)
    head_terms = jnp.dot(attended, output_weight, preferred_element_type=jnp.float32)
    low_part = jnp.einsum(
        "rsc,rkc->rsk",
        attended.reshape(request_number, request_slot_rows, -1),
        output_down_picked,
        preferred_element_type=jnp.float32,
    )
    reduced_output = (
        lax.psum(low_part.reshape(-1, 128).astype(jnp.bfloat16), "tensor")
        .astype(jnp.float32)
        .reshape(request_number, request_slot_rows, adapter_rank_size)
        .astype(jnp.bfloat16)
    )
    head_total = lax.psum_scatter(
        head_terms.astype(jnp.bfloat16), "tensor", scatter_dimension=1, tiled=True
    ).astype(jnp.float32)
    adapter_output = jnp.einsum(
        "ibm,imf->ibf", reduced_output, oup_sel, preferred_element_type=jnp.float32
    ).reshape(row_count, -1)
    return (head_total + ADAPTER_SCALE * adapter_output).astype(jnp.bfloat16)


def solution(mesh):
    placed = (
        P("req", "tensor"),
        P(),
        P(None, "tensor"),
        P(None, "tensor"),
        P("tensor", None),
        P("req", None, "tensor"),
        P("req", None, "tensor"),
        P("req", None, None, "tensor"),
        P("req", None, "tensor"),
        P("req", None, "tensor"),
        P("req"),
        P("req"),
        P(),
        P(),
        P("req", None),
        P("req", None, "tensor"),
    )
    return jax.shard_map(
        local, mesh=mesh, in_specs=placed, out_specs=P("req", "tensor"), check_vma=False
    )
```

profile of v0, /device:TPU:1, one launch (start us, length us, event | category | flops | bytes accessed | tf_op | source)
XLA Modules:
  0.0 329.6 jit_solution(5925808227693249332)
XLA Ops:
  6.5 0.7 all-gather.10.cloned.1.call-update
  7.3 0.7 all-gather.8.cloned.1.call-update
  8.1 0.7 all-gather.6.cloned.1.call-update
  8.8 0.5 all-gather.12.cloned.1.call-update
  9.3 0.5 broadcast.279
  9.9 1.3 reduce.11
  11.5 2.0 gather_fusion
  13.5 3.1 copy.81
  16.6 8.6 %all-to-all-start = ((bf16[2,16,128,256]{3,2,0,1:T(8,128)(2,1)}), bf16[2,16,128,256]{3,2,0,1:T(8,128)(2,1)S(1)}, u32[]{:S(2)}, u32[]{:S(2)}) async-start(bf16[2,16,128,256]{3,2,0,1:T(8,128)(2,1)} %copy.81), calls=%async_computation | async-start | bytes 4194304 | tf_op jit(solution)/shard_map/all_to_all | solution.py:165
  25.2 0.5 all-gather.14.cloned.1.call-update
  26.3 43.4 %all_gather.21 = bf16[64,2,16,128]{3,2,1,0:T(8,128)(2,1)S(1)} all-gather(bf16[4,2,16,128]{3,2,1,0:T(8,128)(2,1)S(1)} %copy-done.7), channel_id=1, replica_groups=mesh['req'=16,'tensor'=8] {'req'}, dimensions={0}, use_global_device_ids=true | all-gather | bytes 557056 | tf_op jit(solution)/shard_map/all_gather | solution.py:95
  70.7 0.6 slice_bitcast_fusion.4
  71.5 1.8 multiply_cosine_fusion
  73.3 2.4 convolution_convert_fusion.2
  75.8 1.5 copy.82
  77.3 54.5 %all-gather.8.cloned.1.call-done = bf16[64,48,896]{2,1,0:T(8,128)(2,1)} async-done(((bf16[4,48,896]{2,1,0:T(8,128)(2,1)}), bf16[64,48,896]{2,1,0:T(8,128)(2,1)}) %all-gather.8.cloned.1.call-update) | async-done | bytes 5505040 | tf_op jit(solution)/shard_map/all_gather | solution.py:93
  131.8 3.8 %fusion.25 = bf16[4,48,896]{2,0,1:T(4,128)(2,1)S(1)} fusion(s32[4]{0:T(128)S(1)} %copy-done.11, bf16[8,8,48,896]{3,2,1,0:T(8,128)(2,1)} %bitcast.206), kind=kOutput, calls=%fused_computation.33 | convolution fusion | flops 22192384 | bytes 5849104 | tf_op jit(solution)/shard_map/dot_general | solution.py:104
  135.6 43.3 %all-gather.6.cloned.1.call-done = bf16[512,7168]{1,0:T(8,128)(2,1)} async-done(((bf16[512,896]{1,0:T(8,128)(2,1)}), bf16[512,7168]{1,0:T(8,128)(2,1)}) %all-gather.6.cloned.1.call-update) | async-done | bytes 7340048 | tf_op jit(solution)/shard_map/all_gather | solution.py:76
  178.9 4.7 %fusion = f32[512]{0:T(512)S(1)} fusion(bf16[512,7168]{1,0:T(8,128)(2,1)} %all-gather.6.cloned.1.call-done), kind=kLoop, calls=%fused_computation.3 | loop fusion | flops 11009536 | bytes 7342080 | tf_op jit(solution)/shard_map/reduce_sum | solution.py:78
  183.6 0.4 copy-done.3
  184.0 5.8 %fusion.2 = bf16[512,7168]{1,0:T(8,128)(2,1)} fusion(bf16[512,7168]{1,0:T(8,128)(2,1)S(1)} %copy-done.3, f32[7168]{0:T(1024)S(1)} %copy-done.8, f32[512]{0:T(512)S(1)} %add_rsqrt_fusion), kind=kLoop, calls=%fused_computation.5 | loop fusion | flops 14680064 | bytes 14710784 | tf_op jit(solution)/shard_map/convert_element_type | solution.py:79
  189.8 1.3 constant_dynamic-slice_fusion
  191.1 0.5 convolution_convert_fusion.3
  191.5 21.7 %psum.14 = bf16[4,128,48]{1,2,0:T(8,128)(2,1)S(1)} all-reduce(bf16[4,128,48]{1,2,0:T(8,128)(2,1)S(1)} %convolution_convert_fusion.3), channel_id=1, replica_groups=mesh['req'=16,'tensor'=8] {'tensor'}, use_global_device_ids=true, to_apply=%region_1.0 | all-reduce | flops 24576 | bytes 98304 | tf_op jit(solution)/shard_map/psum | solution.py:118
  213.2 8.6 %fusion.102 = f32[512,512]{1,0:T(8,128)S(1)} fusion(bf16[512,7168]{1,0:T(8,128)(2,1)} %fusion.2, bf16[7168,512]{1,0:T(8,128)(2,1)} %param.18), kind=kOutput, calls=%fused_computation.141 | convolution fusion | flops 3758096384 | bytes 15728640 | tf_op jit(solution)/shard_map/dot_general | solution.py:123
  222.5 0.6 fusion.100
  223.1 6.3 %fusion.103 = f32[512,256]{1,0:T(8,128)S(1)} fusion(bf16[512,7168]{1,0:T(8,128)(2,1)} %fusion.2, bf16[7168,256]{1,0:T(8,128)(2,1)} %param.19), kind=kOutput, calls=%fused_computation.142 | convolution fusion | flops 1879048192 | bytes 11534336 | tf_op jit(solution)/shard_map/dot_general | solution.py:132
  230.1 1.5 fusion.3
  231.6 3.2 copy-done.2
  234.9 2.8 fusion.4
  237.6 0.7 slice.61
  238.4 1.1 copy.109
  239.4 0.7 stack.31
  240.1 4.6 %fusion.22 = f32[2,1,1,128,4,128]{3,5,4,1,0,2:T(8,128)S(1)} fusion(f32[2,128,4,2048]{3,1,2,0:T(8,128)} %copy-done.2, f32[2,128,4]{1,2,0:T(4,128)S(1)} %get-tuple-element.18, pred[2,2048]{1,0:T(4,128)(4,1)S(1)} %fusion.71, bf16[2,2048,1,256]{3,1,0,2:T(8,128)(2,1)S(1)} %bitcast.191), kind=kOutput, calls=%fused_computation.32 | convolution fusion | flops 547356672 | bytes 9973760 | tf_op jit(solution)/shard_map/bvsgk,bkvd->bvsgd/dot_general | solution.py:38
  245.1 0.6 fusion.70
  245.7 0.5 fusion.101
  246.4 1.1 bitcast_multiply_fusion
  247.5 1.9 fusion.21
  249.7 9.4 %convolution_convert_fusion = bf16[512,7168]{1,0:T(8,128)(2,1)} fusion(bf16[512,7168]{1,0:T(8,128)(2,1)} %param.20, bf16[64,8,4,128]{3,2,1,0:T(4,128)(2,1)S(1)} %bitcast.200), kind=kOutput, calls=%fused_computation.6 | convolution fusion | flops 3761766400 | bytes 15204352 | tf_op jit(solution)/shard_map/dot_general | solution.py:197
  259.2 10.5 %copy.105 = bf16[512,7168]{0,1:T(8,128)(2,1)} copy(bf16[512,7168]{1,0:T(8,128)(2,1)} %convolution_convert_fusion) | data formatting | bytes 14680064
  269.7 0.6 copy-done.12
  270.3 2.5 convolution_convert_fusion.1
  272.7 2.0 fusion.31
  274.9 24.3 %psum.15 = bf16[4,128,16]{1,2,0:T(8,128)(2,1)S(1)} all-reduce(bf16[4,128,16]{1,2,0:T(8,128)(2,1)S(1)} %convolution_convert_fusion.5), channel_id=1, replica_groups=mesh['req'=16,'tensor'=8] {'tensor'}, use_global_device_ids=true, to_apply=%region_7.8 | all-reduce | flops 8192 | bytes 32768 | tf_op jit(solution)/shard_map/psum | solution.py:205
  299.2 1.8 convolution_multiply_fusion
  300.9 17.8 %reduce-scatter.4.cloned.1.call-done = bf16[896,512]{1,0:T(8,128)(2,1)} async-done(((bf16[7168,512]{1,0:T(8,128)(2,1)}), bf16[896,512]{1,0:T(8,128)(2,1)}) %reduce-scatter.4.cloned.1.call-update) | async-done | bytes 917520
  318.7 1.5 copy.106
  320.2 2.6 fusion.15
  (77 shorter events, 4.6 us)
Async XLA Ops:
  6.5 4.9 %copy-start = (bf16[32,128,256]{2,1,0:T(8,128)(2,1)S(1)}, bf16[32,128,256]{2,1,0:T(8,128)(2,1)}, u32[]{:S(2)}) copy-start(bf16[32,128,256]{2,1,0:T(8,128)(2,1)} %param.31) | copy-start | bytes 6291460
  6.5 19.3 %copy-start.16 = (s32[32]{0:T(128)S(1)}, s32[32]{0:T(128)}, u32[]{:S(2)}) copy-start(s32[32]{0:T(128)} %param.28) | copy-start | bytes 388
  6.5 19.7 %copy-start.7 = (bf16[4,2,16,128]{3,2,1,0:T(8,128)(2,1)S(1)}, bf16[4,2,16,128]{3,2,1,0:T(8,128)(2,1)}, u32[]{:S(2)}) copy-start(bf16[4,2,16,128]{3,2,1,0:T(8,128)(2,1)} %param.23) | copy-start | bytes 98308
  6.5 66.8 %all-gather.10.cloned.1.call-start = ((), (), s32[]{:S(2)}) async-start(), calls=%async_computation.4 | async-start | bytes 1114112 | tf_op jit(solution)/shard_map/all_gather | solution.py:94
  7.3 62.4 %copy-start.14 = (s32[4]{0:T(128)S(1)}, s32[4]{0:T(128)}, u32[]{:S(2)}) copy-start(s32[4]{0:T(128)} %param.27) | copy-start | bytes 52
  7.3 62.5 %copy-start.15 = (s32[32]{0:T(128)S(1)}, s32[32]{0:T(128)}, u32[]{:S(2)}) copy-start(s32[32]{0:T(128)} %param.29) | copy-start | bytes 388
  7.3 124.5 %all-gather.8.cloned.1.call-start = ((), (), s32[]{:S(2)}) async-start(), calls=%async_computation.3 | async-start | bytes 5849088 | tf_op jit(solution)/shard_map/all_gather | solution.py:93
  8.0 170.8 %all-gather.6.cloned.1.call-start = ((), (), s32[]{:S(2)}) async-start(), calls=%async_computation.2 | async-start | bytes 8257536 | tf_op jit(solution)/shard_map/all_gather | solution.py:76
  8.8 260.9 %all-gather.12.cloned.1.call-start = ((), (), s32[]{:S(2)}) async-start(), calls=%async_computation.5 | async-start | bytes 1114112 | tf_op jit(solution)/shard_map/all_gather | solution.py:96
  11.5 59.0 %copy-start.11 = (s32[4]{0:T(128)S(1)}, s32[4]{0:T(128)}, u32[]{:S(2)}) copy-start(s32[4]{0:T(128)} %param.26) | copy-start | bytes 52
  16.6 59.2 %all-to-all-start = ((bf16[2,16,128,256]{3,2,0,1:T(8,128)(2,1)}), bf16[2,16,128,256]{3,2,0,1:T(8,128)(2,1)S(1)}, u32[]{:S(2)}, u32[]{:S(2)}) async-start(bf16[2,16,128,256]{3,2,0,1:T(8,128)(2,1)} %copy.81), calls=%async_computation | async-start | bytes 4194304 | tf_op jit(solution)/shard_map/all_to_all | solution.py:165
  25.2 247.6 %all-gather.14.cloned.1.call-start = ((), (), s32[]{:S(2)}) async-start(), calls=%async_computation.6 | async-start | bytes 1949696 | tf_op jit(solution)/shard_map/all_gather | solution.py:97
  25.8 292.9 %reduce-scatter.4.cloned.1.call-start = ((), (), s32[]{:S(2)}) async-start(), calls=%async_computation.7 | async-start | bytes 8257536
  69.8 65.8 %copy-start.13 = (pred[4,128]{1,0:T(4,128)(4,1)}, pred[4,128]{1,0:T(4,128)(4,1)S(1)}, u32[]{:S(2)}) copy-start(pred[4,128]{1,0:T(4,128)(4,1)S(1)} %iota_compare_fusion.2) | copy-start | bytes 1540
  70.0 65.6 %copy-start.9 = (f32[64]{0:T(128)}, f32[64]{0:T(128)S(1)}, u32[]{:S(2)}) copy-start(f32[64]{0:T(128)S(1)} %multiply_power_fusion) | copy-start | bytes 772
  131.8 51.8 %copy-start.8 = (f32[7168]{0:T(1024)S(1)}, f32[7168]{0:T(1024)}, u32[]{:S(2)}) copy-start(f32[7168]{0:T(1024)} %param.17) | copy-start | bytes 86020
  178.9 5.2 %copy-start.3 = (bf16[512,7168]{1,0:T(8,128)(2,1)S(1)}, bf16[512,7168]{1,0:T(8,128)(2,1)}, u32[]{:S(2)}) copy-start(bf16[512,7168]{1,0:T(8,128)(2,1)} %all-gather.6.cloned.1.call-done) | copy-start | bytes 22020100
  223.1 6.4 %copy-start.5 = (f32[4,128,64]{2,1,0:T(8,128)S(1)}, f32[4,128,64]{2,1,0:T(8,128)}, u32[]{:S(2)}) copy-start(f32[4,128,64]{2,1,0:T(8,128)} %get-tuple-element.17) | copy-start | bytes 393220
  223.1 7.0 %copy-start.4 = (bf16[2,16,128,256]{3,2,1,0:T(8,128)(2,1)S(1)}, bf16[2,16,128,256]{3,2,1,0:T(8,128)(2,1)}, u32[]{:S(2)}) copy-start(bf16[2,16,128,256]{3,2,1,0:T(8,128)(2,1)} %copy.82) | copy-start | bytes 6291460
  229.5 8.2 %copy-start.6 = (f32[512,256]{1,0:T(8,128)}, f32[512,256]{1,0:T(8,128)S(1)}, u32[]{:S(2)}) copy-start(f32[512,256]{1,0:T(8,128)S(1)} %fusion.103) | copy-start | bytes 1572868
  231.6 3.2 copy-start.2
  240.1 5.0 %copy-start.10 = (f32[64]{0:T(128)S(1)}, f32[64]{0:T(128)}, u32[]{:S(2)}) copy-start(f32[64]{0:T(128)} %copy-done.9) | copy-start | bytes 772
  269.6 0.7 copy-start.12
  269.6 53.2 %copy-start.1 = (bf16[32,128,256]{2,1,0:T(8,128)(2,1)S(1)}, bf16[32,128,256]{2,1,0:T(8,128)(2,1)}, u32[]{:S(2)}) copy-start(bf16[32,128,256]{2,1,0:T(8,128)(2,1)} %param.31) | copy-start | bytes 6291460
Sparse Core Ops, SparseCore 0:
  9.5 61.4 all-gather.9
  73.1 58.6 all-gather.7
  133.5 45.3 all-gather.5
  180.8 40.6 all-gather.11
  223.5 44.1 all-gather.13
  270.0 48.6 reduce-scatter.3
where the time goes:
time: 330 us
  waiting for transfers between devices  119 us (36%)
  blocking collectives  89.4 us (27%)
  matrix products  46.7 us (14%)
  local copies, waits for them, and re-layouts  30.3 us (9%)
  other arithmetic  22 us (7%)
  between operations  13.8 us (4%)
  starting transfers between devices  8.78 us (3%)
    all_gather x1, waiting for transfers between devices, local(): lax.all_gather(adapter_down_maps, 'req', axis=0, tiled=True)  54.5 us
    all_gather x1, blocking collectives, local(): lax.all_gather(adapter_key_value_up, 'req', axis=0, tiled=True)  43.4 us
    all_gather x1, waiting for transfers between devices, local(): gathered = lax.all_gather(residual_input, 'tensor', axis=1, tiled=True)  43.3 us
    psum x1, blocking collectives, local(): lax.psum(low_part.reshape(-1, 128).astype(jnp.bfloat16), 'tensor')  24.3 us
    psum x1, blocking collectives, local(): lax.psum(partial_low.reshape(-1, 128).astype(jnp.bfloat16), 'tensor')  21.7 us
    unnamed x7, waiting for transfers between devices  20.9 us
    unnamed x42, local copies, waits for them, and re-layouts  18.3 us
    dot_general x5, matrix products, local(): jnp.dot(onehot, segment.reshape(block_count, -1), preferred_element_type=...  10.9 us
  transfers between devices with their start and end apart: 7, of which 3 were waited for; matrix products, arithmetic and copies ran while one was open for 27% of the time, Pallas kernels for 0%

commit v1 on v0

--- a/solution.py
+++ b/solution.py
@@ -8,6 +8,24 @@
 ADAPTER_SCALE = 2.0
 EPSILON = 1e-05
 NEG_FILL = -1e30
+
+
+def ring_gather(value, axis, dim):
+    ways, here, turn = (lax.axis_size(axis), lax.axis_index(axis), value.shape[dim])
+    lengths = [n * ways if d == dim else n for d, n in enumerate(value.shape)]
+    full = lax.dynamic_update_slice_in_dim(
+        jnp.zeros(lengths, value.dtype), value, here * turn, axis=dim
+    )
+    going_up = going_down = value
+    for far in range(1, ways // 2 + 1):
+        going_up = lax.ppermute(going_up, axis, [(d, (d + 1) % ways) for d in range(ways)])
+        full = lax.dynamic_update_slice_in_dim(full, going_up, (here - far) % ways * turn, axis=dim)
+        if 2 * far < ways:
+            going_down = lax.ppermute(going_down, axis, [(d, (d - 1) % ways) for d in range(ways)])
+            full = lax.dynamic_update_slice_in_dim(
+                full, going_down, (here + far) % ways * turn, axis=dim
+            )
+    return full
 
 
 def rotate(vectors, positions):
@@ -73,7 +91,7 @@
     local_kv = key_value_weight.shape[1] // (2 * HEAD_SIZE)
     group_size = query_weight.shape[1] // (HEAD_SIZE * local_kv)
     page_rows = cache_page_pool.shape[1]
-    gathered = lax.all_gather(residual_input, "tensor", axis=1, tiled=True)
+    gathered = ring_gather(residual_input, "tensor", 1)
     widened = gathered.astype(jnp.float32)
     inverse = lax.rsqrt(jnp.mean(widened * widened, axis=1, keepdims=True) + EPSILON)
     normed = (widened * inverse * input_norm_gain).astype(jnp.bfloat16)

time: 330 us -> 282 us (0.85)
  waiting for transfers between devices: 119 us -> 40.8 us
  local copies, waits for them, and re-layouts: 30.3 us -> 44.3 us
  starting transfers between devices: 8.78 us -> 22.7 us
    all_gather x1, waiting for transfers between devices: 54.5 us -> 0.01 us  [local(): lax.all_gather(adapter_down_maps, 'req', axis=0, tiled=True)]
    all_gather x1 -> x0, waiting for transfers between devices: 43.3 us -> none  [local(): gathered = lax.all_gather(residual_input, 'tensor', axis=1, tiled=True)]
    dynamic_update_slice x0 -> x8, local copies, waits for them, and re-layouts: none -> 15.6 us  [the longest x4 7.82 us: ring_gather(): lax.dynamic_update_slice_in_dim(full, going_up, (here - far) % ways * tur...]
    ppermute x0 -> x7, starting transfers between devices: none -> 14.6 us  [the longest x4 14.6 us: ring_gather(): lax.ppermute(going_up, axis, [(d, (d + 1) % ways) for d in range(ways)])]
    ppermute x0 -> x7, waiting for transfers between devices: none -> 9.49 us  [the longest x4 9.41 us: ring_gather(): lax.ppermute(going_up, axis, [(d, (d + 1) % ways) for d in range(ways)])]
    all_gather x1, waiting for transfers between devices: 0.01 us -> 5.49 us  [local(): lax.all_gather(adapter_output_up, 'req', axis=0, tiled=True)]
    unnamed x7 -> x6, waiting for transfers between devices: 20.9 us -> 25.8 us
    unnamed x42 -> x38, local copies, waits for them, and re-layouts: 18.3 us -> 14.3 us
  transfers between devices with their start and end apart: 7 -> 13, of which waited for: 3 -> 5; matrix products, arithmetic and copies ran while one was open for 27% -> 40% of each run, Pallas kernels for 0% -> 0%
where the time goes in v1:
time: 282 us; the launch traced here: 281 us
  blocking collectives  88.2 us (31%)
  matrix products  47.6 us (17%)
  local copies, waits for them, and re-layouts  44.3 us (16%)
  waiting for transfers between devices  40.8 us (14%)
  other arithmetic  24 us (9%)
  starting transfers between devices  22.7 us (8%)
  between operations  13.5 us (5%)
    all_gather x1, blocking collectives, local(): lax.all_gather(adapter_key_value_up, 'req', axis=0, tiled=True)  41.9 us
    unnamed x6, waiting for transfers between devices  25.8 us
    psum x1, blocking collectives, local(): lax.psum(partial_low.reshape(-1, 128).astype(jnp.bfloat16), 'tensor')  23.4 us
    psum x1, blocking collectives, local(): lax.psum(low_part.reshape(-1, 128).astype(jnp.bfloat16), 'tensor')  22.9 us
    ppermute x4, starting transfers between devices, ring_gather(): lax.ppermute(going_up, axis, [(d, (d + 1) % ways) for d in range(ways)])  14.6 us
    unnamed x38, local copies, waits for them, and re-layouts  14.3 us
    dot_general x5, matrix products, local(): jnp.dot(onehot, segment.reshape(block_count, -1), preferred_element_type=...  11 us
    dot_general x1, matrix products, local(): jnp.dot(normed, query_weight, preferred_element_type=jnp.float32)  10.3 us
  transfers between devices with their start and end apart: 13, of which 5 were waited for; matrix products, arithmetic and copies ran while one was open for 40% of the time, Pallas kernels for 0%

profile of v1, /device:TPU:1, one launch (start us, length us, event | category | flops | bytes accessed | tf_op | source)
XLA Modules:
  0.0 281.2 jit_solution(17909278081929096319)
XLA Ops:
  8.7 2.6 collective-permute-start
  11.9 1.3 reduce.11
  13.5 2.0 gather_fusion
  15.5 3.1 %copy.81 = bf16[2,16,128,256]{3,2,0,1:T(8,128)(2,1)} copy(bf16[2,16,128,256]{3,2,1,0:T(8,128)(2,1)} %bitcast.184) | data formatting | bytes 4194304 | tf_op jit(solution)/shard_map/reshape | solution.py:180
  18.6 7.9 %all-to-all-start = ((bf16[2,16,128,256]{3,2,0,1:T(8,128)(2,1)}), bf16[2,16,128,256]{3,2,0,1:T(8,128)(2,1)S(1)}, u32[]{:S(2)}, u32[]{:S(2)}) async-start(bf16[2,16,128,256]{3,2,0,1:T(8,128)(2,1)} %copy.81), calls=%async_computation | async-start | bytes 4194304 | tf_op jit(solution)/shard_map/all_to_all | solution.py:183
  27.2 41.9 %all_gather.17 = bf16[64,2,16,128]{3,2,1,0:T(8,128)(2,1)S(1)} all-gather(bf16[4,2,16,128]{3,2,1,0:T(8,128)(2,1)} %param.23), channel_id=1, replica_groups=mesh['req'=16,'tensor'=8] {'req'}, dimensions={0}, use_global_device_ids=true | all-gather | bytes 557056 | tf_op jit(solution)/shard_map/all_gather | solution.py:113
  71.5 7.2 %collective-permute-start.2 = (bf16[512,896]{1,0:T(8,128)(2,1)}, bf16[512,896]{1,0:T(8,128)(2,1)}, u32[]{:S(2)}, u32[]{:S(2)}) collective-permute-start(bf16[512,896]{1,0:T(8,128)(2,1)} %collective-permute-done), channel_id=1, source_target_pairs={{0,1},{1,2},{2,3},{3,4},{4,5},{5,6},{6,7},{7,0},{8,9},{9,10},{10,1... | collective-permute-start | bytes 2752520 | tf_op jit(solution)/shard_map/ppermute | solution.py:21
  79.5 0.8 broadcast_and_fusion
  80.2 3.8 %broadcast_in_dim.46 = bf16[512,7168]{1,0:T(8,128)(2,1)} broadcast(bf16[]{:T(256)} %constant.85.clone.1), dimensions={} | broadcast | bytes 7340034 | tf_op jit(solution)/shard_map/broadcast_in_dim | solution.py:17
  84.1 1.1 constant_dynamic-update-slice_fusion.7
  85.2 1.2 dynamic_slice.10
  86.4 2.9 %collective-permute-done.2 = bf16[512,896]{1,0:T(8,128)(2,1)} collective-permute-done((bf16[512,896]{1,0:T(8,128)(2,1)}, bf16[512,896]{1,0:T(8,128)(2,1)}, u32[]{:S(2)}, u32[]{:S(2)}) %collective-permute-start.2) | collective-permute-done | bytes 917536 | tf_op jit(solution)/shard_map/ppermute | solution.py:21
  89.3 2.5 collective-permute-start.4
  91.8 1.0 multiply_cosine_fusion
  92.8 0.8 fusion.69
  93.7 2.2 constant_dynamic-update-slice_fusion.6
  95.9 6.6 %collective-permute-done.4 = bf16[512,896]{1,0:T(8,128)(2,1)S(1)} collective-permute-done((bf16[512,896]{1,0:T(8,128)(2,1)}, bf16[512,896]{1,0:T(8,128)(2,1)S(1)}, u32[]{:S(2)}, u32[]{:S(2)}) %collective-permute-start.4) | collective-permute-done | bytes 917536 | tf_op jit(solution)/shard_map/ppermute | solution.py:21
  102.4 2.4 collective-permute-start.6
  104.8 2.2 constant_dynamic-update-slice_fusion.5
  107.0 2.2 constant_dynamic-update-slice_fusion.4
  109.3 2.2 constant_dynamic-update-slice_fusion.3
  111.5 1.5 copy.82
  113.0 2.5 convolution_convert_fusion.2
  115.5 1.1 constant_dynamic-update-slice_fusion.2
  116.6 2.2 constant_dynamic-update-slice_fusion.1
  118.8 2.3 constant_dynamic-update-slice_fusion
  121.1 4.7 %fusion = f32[512]{0:T(512)S(1)} fusion(bf16[512,7168]{1,0:T(8,128)(2,1)} %constant_dynamic-update-slice_fusion), kind=kLoop, calls=%fused_computation.3 | loop fusion | flops 11009536 | bytes 7342080 | tf_op jit(solution)/shard_map/reduce_sum | solution.py:96
  125.9 5.8 %fusion.2 = bf16[512,7168]{1,0:T(8,128)(2,1)S(1)} fusion(bf16[512,7168]{1,0:T(8,128)(2,1)} %constant_dynamic-update-slice_fusion, f32[7168]{0:T(1024)S(1)} %copy-done.7, f32[512]{0:T(512)S(1)} %add_rsqrt_fusion), kind=kLoop, calls=%fused_computation.5 | loop fusion | flops 14680064 | bytes 14710784 | tf_op jit(solution)/shard_map/convert_element_type | solution.py:97
  131.8 6.7 %fusion.101 = f32[512,256]{1,0:T(8,128)S(1)} fusion(bf16[512,7168]{1,0:T(8,128)(2,1)S(1)} %fusion.2, bf16[7168,256]{1,0:T(8,128)(2,1)} %param.19), kind=kOutput, calls=%fused_computation.148 | convolution fusion | flops 1879048192 | bytes 11534336 | tf_op jit(solution)/shard_map/dot_general | solution.py:150
  138.7 10.3 %fusion.100 = f32[512,512]{1,0:T(8,128)} fusion(bf16[512,7168]{1,0:T(8,128)(2,1)} %copy-done.2, bf16[7168,512]{1,0:T(8,128)(2,1)} %param.18), kind=kOutput, calls=%fused_computation.147 | convolution fusion | flops 3758096384 | bytes 15728640 | tf_op jit(solution)/shard_map/dot_general | solution.py:141
  149.0 3.8 %fusion.24 = bf16[4,48,896]{2,0,1:T(4,128)(2,1)S(1)} fusion(s32[4]{0:T(128)S(1)} %copy-done.9, bf16[8,8,48,896]{3,2,1,0:T(8,128)(2,1)} %bitcast.201), kind=kOutput, calls=%fused_computation.32 | convolution fusion | flops 22192384 | bytes 5849104 | tf_op jit(solution)/shard_map/dot_general | solution.py:122
  153.2 23.4 %psum.14 = bf16[4,128,48]{1,2,0:T(8,128)(2,1)S(1)} all-reduce(bf16[4,128,48]{1,2,0:T(8,128)(2,1)S(1)} %convolution_convert_fusion.3), channel_id=1, replica_groups=mesh['req'=16,'tensor'=8] {'tensor'}, use_global_device_ids=true, to_apply=%region_1.2 | all-reduce | flops 24576 | bytes 98304 | tf_op jit(solution)/shard_map/psum | solution.py:136
  177.0 1.4 add.206
  180.0 2.8 %fusion.3 = (f32[2,128,4]{1,2,0:T(4,128)S(1)}, f32[2,128,4,2048]{3,1,2,0:T(8,128)S(1)}) fusion(pred[2,2048]{1,0:T(4,128)(4,1)S(1)} %fusion.69, bf16[2,2048,1,256]{3,1,0,2:T(8,128)(2,1)} %bitcast.185, bf16[4,128,1,4,128]{4,1,3,0,2:T(8,128)(2,1)S(1)} %pad_maximum_fusion), kind=kOutput, calls=%fused_computation.9 | convolution fusion | flops 543161344 | bytes 9711616 | tf_op jit(solution)/shard_map/bsvgd,bkvd->bvsgk/dot_general | solution.py:48
  182.9 2.2 fusion.4
  185.1 2.3 fusion.21
  189.0 1.1 bitcast_multiply_fusion
  190.2 1.8 fusion.20
  192.3 9.2 %convolution_convert_fusion = bf16[512,7168]{1,0:T(8,128)(2,1)} fusion(bf16[512,7168]{1,0:T(8,128)(2,1)} %param.20, bf16[64,8,4,128]{3,2,1,0:T(4,128)(2,1)S(1)} %bitcast.195), kind=kOutput, calls=%fused_computation.6 | convolution fusion | flops 3761766400 | bytes 15204352 | tf_op jit(solution)/shard_map/dot_general | solution.py:215
  201.5 10.4 %copy.105 = bf16[512,7168]{0,1:T(8,128)(2,1)} copy(bf16[512,7168]{1,0:T(8,128)(2,1)} %convolution_convert_fusion) | data formatting | bytes 14680064
  212.6 2.5 convolution_convert_fusion.1
  215.1 5.5 %all-gather.11.cloned.1.call-done = bf16[64,16,896]{2,1,0:T(8,128)(2,1)} async-done(((bf16[4,16,896]{2,1,0:T(8,128)(2,1)}), bf16[64,16,896]{2,1,0:T(8,128)(2,1)}) %all-gather.11.cloned.1.call-update) | async-done | bytes 1835024 | tf_op jit(solution)/shard_map/all_gather | solution.py:115
  220.6 2.0 fusion.28
  222.7 22.9 %psum.15 = bf16[4,128,16]{1,2,0:T(8,128)(2,1)S(1)} all-reduce(bf16[4,128,16]{1,2,0:T(8,128)(2,1)S(1)} %convolution_convert_fusion.5), channel_id=1, replica_groups=mesh['req'=16,'tensor'=8] {'tensor'}, use_global_device_ids=true, to_apply=%region_7.8 | all-reduce | flops 8192 | bytes 32768 | tf_op jit(solution)/shard_map/psum | solution.py:223
  245.6 1.7 convolution_multiply_fusion
  247.4 23.2 %reduce-scatter.4.cloned.1.call-done = bf16[896,512]{1,0:T(8,128)(2,1)} async-done(((bf16[7168,512]{1,0:T(8,128)(2,1)}), bf16[896,512]{1,0:T(8,128)(2,1)}) %reduce-scatter.4.cloned.1.call-update) | async-done | bytes 917520
  270.5 1.5 copy.106
  272.1 2.6 fusion.15
  (94 shorter events, 12.2 us)
Async XLA Ops:
  6.5 6.9 %copy-start = (bf16[32,128,256]{2,1,0:T(8,128)(2,1)S(1)}, bf16[32,128,256]{2,1,0:T(8,128)(2,1)}, u32[]{:S(2)}) copy-start(bf16[32,128,256]{2,1,0:T(8,128)(2,1)} %param.31) | copy-start | bytes 6291460
  6.5 62.6 %copy-start.14 = (s32[32]{0:T(128)S(1)}, s32[32]{0:T(128)}, u32[]{:S(2)}) copy-start(s32[32]{0:T(128)} %param.28) | copy-start | bytes 388
  6.5 106.5 %all-gather.7.cloned.1.call-start = ((), (), s32[]{:S(2)}) async-start(), calls=%async_computation.3 | async-start | bytes 1114112 | tf_op jit(solution)/shard_map/all_gather | solution.py:112
  7.3 141.7 %all-gather.5.cloned.1.call-start = ((), (), s32[]{:S(2)}) async-start(), calls=%async_computation.2 | async-start | bytes 5849088 | tf_op jit(solution)/shard_map/all_gather | solution.py:111
  8.0 204.0 %all-gather.9.cloned.1.call-start = ((), (), s32[]{:S(2)}) async-start(), calls=%async_computation.4 | async-start | bytes 1114112 | tf_op jit(solution)/shard_map/all_gather | solution.py:114
  8.7 62.7 %collective-permute-start = (bf16[512,896]{1,0:T(8,128)(2,1)}, bf16[512,896]{1,0:T(8,128)(2,1)}, u32[]{:S(2)}, u32[]{:S(2)}) collective-permute-start(bf16[512,896]{1,0:T(8,128)(2,1)} %param.16), channel_id=1, source_target_pairs={{0,1},{1,2},{2,3},{3,4},{4,5},{5,6},{6,7},{7,0},{8,9},{9,10},{10,1... | collective-permute-start | bytes 2752520 | tf_op jit(solution)/shard_map/ppermute | solution.py:21
  11.3 68.9 %collective-permute-start.1 = (bf16[512,896]{1,0:T(8,128)(2,1)}, bf16[512,896]{1,0:T(8,128)(2,1)}, u32[]{:S(2)}, u32[]{:S(2)}) collective-permute-start(bf16[512,896]{1,0:T(8,128)(2,1)} %param.16), channel_id=1, source_target_pairs={{0,7},{1,0},{2,1},{3,2},{4,3},{5,4},{6,5},{7,6},{8,15},{9,8},{10,9... | collective-permute-start | bytes 2752520 | tf_op jit(solution)/shard_map/ppermute | solution.py:24
  13.5 56.3 %copy-start.13 = (s32[32]{0:T(128)S(1)}, s32[32]{0:T(128)}, u32[]{:S(2)}) copy-start(s32[32]{0:T(128)} %param.29) | copy-start | bytes 388
  13.5 56.4 %copy-start.8 = (s32[4]{0:T(128)S(1)}, s32[4]{0:T(128)}, u32[]{:S(2)}) copy-start(s32[4]{0:T(128)} %param.26) | copy-start | bytes 52
  18.6 65.4 %copy-start.4 = (bf16[512,896]{1,0:T(8,128)(2,1)S(1)}, bf16[512,896]{1,0:T(8,128)(2,1)}, u32[]{:S(2)}) copy-start(bf16[512,896]{1,0:T(8,128)(2,1)} %param.16) | copy-start | bytes 2752516
  18.6 92.8 %all-to-all-start = ((bf16[2,16,128,256]{3,2,0,1:T(8,128)(2,1)}), bf16[2,16,128,256]{3,2,0,1:T(8,128)(2,1)S(1)}, u32[]{:S(2)}, u32[]{:S(2)}) async-start(bf16[2,16,128,256]{3,2,0,1:T(8,128)(2,1)} %copy.81), calls=%async_computation | async-start | bytes 4194304 | tf_op jit(solution)/shard_map/all_to_all | solution.py:183
  26.5 194.1 %all-gather.11.cloned.1.call-start = ((), (), s32[]{:S(2)}) async-start(), calls=%async_computation.5 | async-start | bytes 1949696 | tf_op jit(solution)/shard_map/all_gather | solution.py:115
  27.1 243.4 %reduce-scatter.4.cloned.1.call-start = ((), (), s32[]{:S(2)}) async-start(), calls=%async_computation.6 | async-start | bytes 8257536
  71.5 17.8 %collective-permute-start.2 = (bf16[512,896]{1,0:T(8,128)(2,1)}, bf16[512,896]{1,0:T(8,128)(2,1)}, u32[]{:S(2)}, u32[]{:S(2)}) collective-permute-start(bf16[512,896]{1,0:T(8,128)(2,1)} %collective-permute-done), channel_id=1, source_target_pairs={{0,1},{1,2},{2,3},{3,4},{4,5},{5,6},{6,7},{7,0},{8,9},{9,10},{10,1... | collective-permute-start | bytes 2752520 | tf_op jit(solution)/shard_map/ppermute | solution.py:21
  79.4 12.3 %copy-start.11 = (pred[4,128]{1,0:T(4,128)(4,1)}, pred[4,128]{1,0:T(4,128)(4,1)S(1)}, u32[]{:S(2)}) copy-start(pred[4,128]{1,0:T(4,128)(4,1)S(1)} %iota_compare_fusion.2) | copy-start | bytes 1540
  80.2 13.4 %collective-permute-start.3 = (bf16[512,896]{1,0:T(8,128)(2,1)}, bf16[512,896]{1,0:T(8,128)(2,1)}, u32[]{:S(2)}, u32[]{:S(2)}) collective-permute-start(bf16[512,896]{1,0:T(8,128)(2,1)} %collective-permute-done.1), channel_id=1, source_target_pairs={{0,7},{1,0},{2,1},{3,2},{4,3},{5,4},{6,5},{7,6},{8,15},{9,8},{10,9... | collective-permute-start | bytes 2752520 | tf_op jit(solution)/shard_map/ppermute | solution.py:24
  89.3 13.1 %collective-permute-start.4 = (bf16[512,896]{1,0:T(8,128)(2,1)}, bf16[512,896]{1,0:T(8,128)(2,1)S(1)}, u32[]{:S(2)}, u32[]{:S(2)}) collective-permute-start(bf16[512,896]{1,0:T(8,128)(2,1)} %collective-permute-done.2), channel_id=1, source_target_pairs={{0,1},{1,2},{2,3},{3,4},{4,5},{5,6},{6,7},{7,0},{8,9},{9,10},{10,1... | collective-permute-start | bytes 2752520 | tf_op jit(solution)/shard_map/ppermute | solution.py:21
  93.7 22.9 %collective-permute-start.5 = (bf16[512,896]{1,0:T(8,128)(2,1)}, bf16[512,896]{1,0:T(8,128)(2,1)}, u32[]{:S(2)}, u32[]{:S(2)}) collective-permute-start(bf16[512,896]{1,0:T(8,128)(2,1)} %collective-permute-done.3), channel_id=1, source_target_pairs={{0,7},{1,0},{2,1},{3,2},{4,3},{5,4},{6,5},{7,6},{8,15},{9,8},{10,9... | collective-permute-start | bytes 2752520 | tf_op jit(solution)/shard_map/ppermute | solution.py:24
  102.4 16.4 %collective-permute-start.6 = (bf16[512,896]{1,0:T(8,128)(2,1)S(1)}, bf16[512,896]{1,0:T(8,128)(2,1)}, u32[]{:S(2)}, u32[]{:S(2)}) collective-permute-start(bf16[512,896]{1,0:T(8,128)(2,1)S(1)} %collective-permute-done.4), channel_id=1, source_target_pairs={{0,1},{1,2},{2,3},{3,4},{4,5},{5,6},{6,7},{7,0},{8,9},{9,10},{10,1... | collective-permute-start | bytes 2752520 | tf_op jit(solution)/shard_map/ppermute | solution.py:21
  113.0 12.9 %copy-start.7 = (f32[7168]{0:T(1024)S(1)}, f32[7168]{0:T(1024)}, u32[]{:S(2)}) copy-start(f32[7168]{0:T(1024)} %param.17) | copy-start | bytes 86020
  131.7 6.8 %copy-start.2 = (bf16[512,7168]{1,0:T(8,128)(2,1)}, bf16[512,7168]{1,0:T(8,128)(2,1)S(1)}, u32[]{:S(2)}) copy-start(bf16[512,7168]{1,0:T(8,128)(2,1)S(1)} %fusion.2) | copy-start | bytes 22020100
  138.6 10.3 %copy-start.9 = (s32[4]{0:T(128)S(1)}, s32[4]{0:T(128)}, u32[]{:S(2)}) copy-start(s32[4]{0:T(128)} %param.26) | copy-start | bytes 52
  180.0 5.1 %copy-start.3 = (bf16[2,16,128,256]{3,2,1,0:T(8,128)(2,1)S(1)}, bf16[2,16,128,256]{3,2,1,0:T(8,128)(2,1)}, u32[]{:S(2)}) copy-start(bf16[2,16,128,256]{3,2,1,0:T(8,128)(2,1)} %copy.82) | copy-start | bytes 6291460
  185.1 2.4 copy-start.6
  185.1 3.2 %copy-start.5 = (pred[4,128,128]{1,2,0:T(8,128)(4,1)S(1)}, pred[4,128,128]{1,2,0:T(8,128)(4,1)}, u32[]{:S(2)}) copy-start(pred[4,128,128]{1,2,0:T(8,128)(4,1)} %broadcast_and_fusion) | copy-start | bytes 196612
  187.4 2.8 copy-start.12
  211.9 0.7 copy-start.10
  212.0 62.7 %copy-start.1 = (bf16[32,128,256]{2,1,0:T(8,128)(2,1)S(1)}, bf16[32,128,256]{2,1,0:T(8,128)(2,1)}, u32[]{:S(2)}) copy-start(bf16[32,128,256]{2,1,0:T(8,128)(2,1)} %param.31) | copy-start | bytes 6291460
Sparse Core Ops, SparseCore 0:
  9.5 61.2 all-gather.6
  72.9 58.6 all-gather.4
  133.7 40.6 all-gather.8
  176.4 44.1 all-gather.10
  222.9 47.6 reduce-scatter.3
